TPU v7x, 256 devices: a whole 4x4x8 slice. The times are simulated.
256 devices in a mesh: tm: 64 (over z, x_hi, y), chan: 4 (over x_lo, core).
Axes of the slice: x: 4 (x_hi: 2, x_lo: 2; x = x_hi * 2 + x_lo), y: 4, z: 8, core: 2. Of those that a mesh axis runs over, the one named last changes fastest.
Arguments:
- signal: float32 [256, 8192], P('chan', 'tm'), may hold values from -256 to 256
- support: int32 [32], replicated, may hold values from 1 to 4, as said below
- pair_first: int32 [4, 512], replicated, may hold values from 0 to 255
- pair_second: int32 [4, 512], replicated, may hold values from 0 to 255
- pair_count: int32 [4], replicated, may hold values from 128 to 512, as said below
Outputs:
- cross: float32 [4, 512, 2, 32], P('chan', 'tm')
- coherence: float32 [4, 512, 32], P('chan', 'tm')
Inputs may be any that keep to these rules, and one draw needn't show every extreme that they name: With b = q // 8 the band of scale q, support[q] is at most (4 * 128 / 4^(3 - b) + 127) // 128, and equals it for the last scale of every band. The live slots of an owner are its first pair_count slots; some owner has all 512 slots live.
All inputs are finite; a program needn't handle non-finite values.
Results may differ from a plain program's by a relative error of at most 0.0027.
Values may be sent and summed in bfloat16 or wider, within the bound.
No kernel may reach another device: no remote copies, remote signals or barrier semaphores. Data moves between devices by JAX's collectives and lax.ppermute only.
A program may use at most 192 MiB of HBM per device.

v0:
```python
import math
import jax
import jax.numpy as jnp
import numpy as np
from jax import lax
from jax.sharding import PartitionSpec as P

NS = 32
BLK = 128
TD = 128
power_floor = 1e-06


def from_behind(array, axis, by):
    peers = lax.axis_size(axis)
    return lax.ppermute(array, axis, [(i, (i + by) % peers) for i in range(peers)])


def morlet_parts(offset, scale_index, reach_blocks):
    scale_width = 2.0 * TD * jnp.exp2((scale_index - (NS - 1)).astype(jnp.float32) / 4.0)
    scaled_offset = offset.astype(jnp.float32) / scale_width
    amplitude = (
        math.pi ** (-0.25) * lax.rsqrt(scale_width) * jnp.exp(-0.5 * scaled_offset * scaled_offset)
    )
    inside = jnp.abs(offset) < reach_blocks * BLK
    real_part = jnp.where(inside, amplitude * jnp.cos(6.0 * scaled_offset), 0.0)
    imag_part = jnp.where(inside, amplitude * jnp.sin(6.0 * scaled_offset), 0.0)
    return (real_part.astype(jnp.bfloat16), imag_part.astype(jnp.bfloat16))


def wavelet_band(extended, scale_ids, reaches, offsets, time_span):
    channels = extended.shape[0]
    blocks = time_span // BLK
    centre = 4 * time_span // BLK
    tap_blocks = 2 * offsets + 1
    pieces = [
        extended[:, (centre + offset_step) * BLK : (centre + offset_step) * BLK + time_span]
        for offset_step in range(-offsets, offsets + 1)
    ]
    unfolded = jnp.stack(pieces, axis=1).reshape(channels, tap_blocks, blocks, BLK)
    unfolded = unfolded.transpose(0, 2, 1, 3).reshape(channels * blocks, tap_blocks * BLK)
    lag_start = (jnp.arange(tap_blocks, dtype=jnp.int32) - offsets) * BLK
    within = jnp.arange(BLK, dtype=jnp.int32)
    tap_offset = lag_start[:, None, None] + within[None, :, None] - within[None, None, :]

    def single_scale(scale_index, reach_blocks):
        return morlet_parts(tap_offset, scale_index, reach_blocks)

    real_part, imag_part = jax.vmap(single_scale)(scale_ids, reaches)
    kernel_table = jnp.stack([real_part, imag_part], axis=1)
    kernel_table = kernel_table.transpose(2, 3, 0, 1, 4).reshape(tap_blocks * BLK, -1)
    coefficients = jnp.dot(unfolded, kernel_table, preferred_element_type=jnp.float32)
    scale_count = scale_ids.shape[0]
    coefficients = coefficients.astype(jnp.bfloat16).reshape(channels, blocks, scale_count, 2, BLK)
    return coefficients.transpose(2, 3, 0, 1, 4).reshape(scale_count, 2 * channels, time_span)


def pair_spectra(coefficients, flat_index):
    channels = coefficients.shape[1] // 2
    scale_count = coefficients.shape[0]
    gram_matrix = jnp.einsum(
        "qat,qbt->qab", coefficients, coefficients, preferred_element_type=jnp.float32
    )
    real_part = gram_matrix[:, :channels, :channels] + gram_matrix[:, channels:, channels:]
    imag_part = gram_matrix[:, channels:, :channels] - gram_matrix[:, :channels, channels:]
    auto_power = jnp.diagonal(real_part, axis1=1, axis2=2)
    real_pairs = jnp.take(real_part.reshape(scale_count, -1), flat_index, axis=1)
    imag_pairs = jnp.take(imag_part.reshape(scale_count, -1), flat_index, axis=1)
    return (real_pairs, imag_pairs, auto_power)


def shards(signal, support, pair_first, pair_second, pair_count):
    groups = lax.axis_size("chan")
    cluster_number = lax.axis_index("chan")
    time_index = lax.axis_index("tm")
    time_devices = lax.axis_size("tm")
    time_span = signal.shape[1]
    ntime = time_span * time_devices
    rounded = signal.astype(jnp.bfloat16)
    gathered = lax.all_gather(rounded, "chan", axis=0, tiled=True)
    neighbours = [
        from_behind(gathered, "tm", distance) for distance in (4, 3, 2, 1, -1, -2, -3, -4)
    ]
    extended = jnp.concatenate(neighbours[:4] + [gathered] + neighbours[4:], axis=1)
    channels = extended.shape[0]
    first_flat = pair_first.reshape(-1)
    second_flat = pair_second.reshape(-1)
    flat_index = first_flat * channels + second_flat
    per_group = NS // groups
    scale_ids = cluster_number * per_group + jnp.arange(per_group, dtype=jnp.int32)
    coefficients = wavelet_band(
        extended, scale_ids, support[scale_ids], 4 * time_span // BLK, time_span
    )
    real_pairs, imag_pairs, auto_power = pair_spectra(coefficients, flat_index)
    position = np.arange(NS)
    owner_devices = pair_first.shape[0]
    slots_total = pair_first.shape[1]
    stacked = jnp.stack([real_pairs, imag_pairs], axis=0)
    columns = stacked.shape[0]
    partial_value = stacked.reshape(columns, per_group, owner_devices, slots_total).transpose(
        2, 3, 0, 1
    )
    summed = lax.psum_scatter(partial_value, "tm", scatter_dimension=1, tiled=True)
    owned = lax.all_to_all(summed, "chan", split_axis=0, concat_axis=3, tiled=True)
    owned = owned[:, :, :, position] / ntime
    slots_local = owned.shape[1]
    slot_index = time_index * slots_local + jnp.arange(slots_local, dtype=jnp.int32)
    alive_mask = slot_index < pair_count[cluster_number]
    cross_real = owned[0, :, 0, :]
    cross_imag = owned[0, :, 1, :]
    power_total = lax.psum(auto_power, "tm")
    power_groups = lax.all_gather(power_total, "chan", axis=0, tiled=True)
    power_all = power_groups[position] / ntime
    first_row = lax.dynamic_index_in_dim(pair_first, cluster_number, 0, False)
    second_row = lax.dynamic_index_in_dim(pair_second, cluster_number, 0, False)
    first_owned = lax.dynamic_slice_in_dim(first_row, time_index * slots_local, slots_local)
    second_owned = lax.dynamic_slice_in_dim(second_row, time_index * slots_local, slots_local)
    first_power = power_all[:, first_owned].T
    second_power = power_all[:, second_owned].T
    coherence = (cross_real * cross_real + cross_imag * cross_imag) / (
        (first_power + power_floor) * (second_power + power_floor)
    )
    coherence = jnp.where(alive_mask[:, None], coherence, 0.0)[None]
    cross = jnp.stack([cross_real, cross_imag], axis=1)
    cross = jnp.where(alive_mask[:, None, None], cross, 0.0)[None]
    return (cross, coherence.astype(jnp.float32))


def solution(mesh):
    in_specs = (P("chan", "tm"), P(), P(), P(), P())
    out_specs = (P("chan", "tm", None, None), P("chan", "tm", None))
    return jax.shard_map(shards, mesh=mesh, in_specs=in_specs, out_specs=out_specs, check_vma=False)
```

profile of v0, /device:TPU:1, one launch (start us, length us, event | category | flops | bytes accessed | tf_op | source)
XLA Modules:
  0.0 1023.3 jit_solution(1796853218506428714)
XLA Ops:
  8.0 8.3 all_gather.6
  16.4 6.4 collective-permute-start.7
  24.0 5.5 collective-permute-start.5
  32.9 1.2 dynamic_slice.16
  35.2 147.0 %fusion.2 = (bf16[8,1,9,128,128]{4,1,0,3,2:T(2,128)(2,1)S(1)}, bf16[8,1,9,128,128]{4,1,0,3,2:T(2,128)(2,1)S(1)}) fusion(s32[9,128,128]{2,1,0:T(8,128)S(1)} %get-tuple-element.16, s32[8]{0:T(128)S(1)} %broadcast_multiply_fusion.1, f32[8]{0:T(128)S(1)} %get-tuple-element.20, f32[9,128,128]{2,1,0:T(8,128)S(1)} %get-tuple-element.15, f32[8]{0:T(128)S(1)} %get-tuple-element.19), kind=kLoop, calls=%fused_computation.13 | loop fusion | flops 14155776 | bytes 5898336 | tf_op jit(solution)/shard_map/vmap()/convert_element_type | solution.py:28
  182.2 11.7 %maximum_bitcast_fusion = bf16[9,128,8,2,128]{4,3,2,1,0:T(2,128)(2,1)} fusion(bf16[8,1,9,128,128]{4,1,0,3,2:T(2,128)(2,1)S(1)} %get-tuple-element.14, bf16[8,1,9,128,128]{4,1,0,3,2:T(2,128)(2,1)S(1)} %get-tuple-element.13), kind=kLoop, calls=%fused_computation.15 | loop fusion | flops 9437184 | bytes 9437184 | tf_op jit(solution)/shard_map/transpose | solution.py:51
  193.9 8.8 reshape.232
  204.2 7.6 collective-permute-done.1
  211.8 9.1 collective-permute-done.2
  221.3 8.4 collective-permute-done.3
  229.9 3.9 convolution_convert_fusion
  234.8 1.3 fusion.13
  236.0 1.9 slice_add_fusion
  237.9 17.3 %copy.84 = f32[8,256,256]{0,2,1:T(8,128)} copy(f32[8,256,256]{2,1,0:T(8,128)} %get-tuple-element.11) | data formatting | bytes 4194304 | tf_op jit(solution)/shard_map/reshape | solution.py:67
  255.2 16.2 %copy.85 = f32[8,256,256]{0,2,1:T(8,128)} copy(f32[8,256,256]{2,1,0:T(8,128)S(1)} %get-tuple-element.12) | data formatting | bytes 4194304 | tf_op jit(solution)/shard_map/reshape | solution.py:68
  271.4 16.0 %gather_fusion.6 = f32[2048,8]{1,0:T(8,128)S(1)} fusion(f32[8,65536]{0,1:T(8,128)} %bitcast.81, s32[2048]{0:T(1024)S(1)} %fusion.9), kind=kCustom, calls=%fused_computation.clone | custom fusion | bytes 139264 | tf_op jit(solution)/shard_map/jit(_take)/gather | solution.py:67
  287.4 16.0 %gather_fusion.7 = f32[2048,8]{1,0:T(8,128)S(1)} fusion(f32[8,65536]{0,1:T(8,128)} %bitcast.82, s32[2048]{0:T(1024)S(1)} %fusion.9), kind=kCustom, calls=%fused_computation.1.clone | custom fusion | bytes 139264 | tf_op jit(solution)/shard_map/jit(_take)/gather | solution.py:68
  305.1 1.9 maximum_bitcast_fusion.1
  307.8 2.3 gather_fusion.2
  310.1 299.8 %psum.7 = f32[8,256]{0,1:T(8,128)S(1)} all-reduce(f32[8,256]{0,1:T(8,128)S(1)} %bitcast.88), channel_id=1, replica_groups=mesh['tm'=64,'chan'=4] {'tm'}, use_global_device_ids=true, to_apply=%region_1.3 | all-reduce | flops 2048 | bytes 16384 | tf_op jit(solution)/shard_map/psum | solution.py:111
  609.9 61.3 %all_gather.7 = f32[32,256]{1,0:T(8,128)S(1)} all-gather(f32[8,256]{1,0:T(8,128)S(1)} %copy.77), channel_id=1, replica_groups=mesh['tm'=64,'chan'=4] {'chan'}, dimensions={0}, use_global_device_ids=true | all-gather | bytes 40960 | tf_op jit(solution)/shard_map/all_gather | solution.py:112
  671.8 287.3 %all-reduce.3.cloned.1.call-done = f32[4,512,2,8]{3,0,1,2:T(4,128)} async-done(((f32[4,512,2,8]{3,0,1,2:T(4,128)}), f32[4,512,2,8]{3,0,1,2:T(4,128)}) %all-reduce.3.cloned.1.call-update) | async-done | bytes 131088
  960.5 49.6 %all-to-all-start = ((f32[4,1,128]{2,1,0:T(1,128)}), f32[4,1,128]{2,1,0:T(1,128)S(1)}, u32[]{:S(2)}, u32[]{:S(2)}) async-start(f32[4,1,128]{2,1,0:T(1,128)} %reshape.313), calls=%async_computation | async-start | bytes 4096 | tf_op jit(solution)/shard_map/all_to_all | solution.py:104
  1011.4 1.6 all-to-all-done
  (78 shorter events, 17.9 us)
Async XLA Ops:
  7.2 27.0 %copy-start = (s32[32]{0:T(128)S(1)}, s32[32]{0:T(128)}, u32[]{:S(2)}) copy-start(s32[32]{0:T(128)} %param.11) | copy-start | bytes 388
  7.2 951.8 %all-reduce.3.cloned.1.call-start = ((), (), s32[]{:S(2)}) async-start(), calls=%async_computation.1 | async-start | bytes 4194304
  16.4 213.4 %collective-permute-start.7 = (bf16[256,128]{0,1:T(8,128)(2,1)S(1)}, bf16[256,128]{0,1:T(8,128)(2,1)S(1)}, u32[]{:S(2)}, u32[]{:S(2)}) collective-permute-start(bf16[256,128]{0,1:T(8,128)(2,1)S(1)} %copy.59), channel_id=1, source_target_pairs={{0,240},{4,244},{8,248},{12,252},{16,0},{20,4},{24,8},{28,12},{32,... | collective-permute-start | bytes 196616 | tf_op jit(solution)/shard_map/ppermute | solution.py:16
  22.8 207.0 %collective-permute-start.6 = (bf16[256,128]{0,1:T(8,128)(2,1)S(1)}, bf16[256,128]{0,1:T(8,128)(2,1)S(1)}, u32[]{:S(2)}, u32[]{:S(2)}) collective-permute-start(bf16[256,128]{0,1:T(8,128)(2,1)S(1)} %copy.59), channel_id=1, source_target_pairs={{0,244},{4,248},{8,252},{12,0},{16,4},{20,8},{24,12},{28,16},{32,2... | collective-permute-start | bytes 196616 | tf_op jit(solution)/shard_map/ppermute | solution.py:16
  24.0 205.8 %collective-permute-start.5 = (bf16[256,128]{0,1:T(8,128)(2,1)S(1)}, bf16[256,128]{0,1:T(8,128)(2,1)S(1)}, u32[]{:S(2)}, u32[]{:S(2)}) collective-permute-start(bf16[256,128]{0,1:T(8,128)(2,1)S(1)} %copy.59), channel_id=1, source_target_pairs={{0,248},{4,252},{8,0},{12,4},{16,8},{20,12},{24,16},{28,20},{32,24... | collective-permute-start | bytes 196616 | tf_op jit(solution)/shard_map/ppermute | solution.py:16
  29.5 200.2 %collective-permute-start.4 = (bf16[256,128]{0,1:T(8,128)(2,1)S(1)}, bf16[256,128]{0,1:T(8,128)(2,1)S(1)}, u32[]{:S(2)}, u32[]{:S(2)}) collective-permute-start(bf16[256,128]{0,1:T(8,128)(2,1)S(1)} %copy.59), channel_id=1, source_target_pairs={{0,252},{4,0},{8,4},{12,8},{16,12},{20,16},{24,20},{28,24},{32,28}... | collective-permute-start | bytes 196616 | tf_op jit(solution)/shard_map/ppermute | solution.py:16
  30.6 173.4 %collective-permute-start = (bf16[256,128]{0,1:T(8,128)(2,1)S(1)}, bf16[256,128]{0,1:T(8,128)(2,1)S(1)}, u32[]{:S(2)}, u32[]{:S(2)}) collective-permute-start(bf16[256,128]{0,1:T(8,128)(2,1)S(1)} %copy.59), channel_id=1, source_target_pairs={{0,16},{4,20},{8,24},{12,28},{16,32},{20,36},{24,40},{28,44},{32,4... | collective-permute-start | bytes 196616 | tf_op jit(solution)/shard_map/ppermute | solution.py:16
  193.9 8.9 copy-start.2
  204.1 7.7 collective-permute-start.1
  211.8 9.1 collective-permute-start.2
  220.9 8.8 collective-permute-start.3
  304.4 712.0 %copy-start.1 = (s32[32]{0:T(128)S(1)}, s32[32]{0:T(128)}, u32[]{:S(2)}) copy-start(s32[32]{0:T(128)} %param.11) | copy-start | bytes 388
  960.5 52.6 %all-to-all-start = ((f32[4,1,128]{2,1,0:T(1,128)}), f32[4,1,128]{2,1,0:T(1,128)S(1)}, u32[]{:S(2)}, u32[]{:S(2)}) async-start(f32[4,1,128]{2,1,0:T(1,128)} %reshape.313), calls=%async_computation | async-start | bytes 4096 | tf_op jit(solution)/shard_map/all_to_all | solution.py:104
Sparse Core Ops, SparseCore 0:
  307.2 651.7 all-reduce.2
where the time goes:
time: 1020 us
  blocking collectives  369 us (36%)
  waiting for transfers between devices  314 us (31%)
  other arithmetic  168 us (16%)
  local copies, waits for them, and re-layouts  87.8 us (9%)
  starting transfers between devices  64.3 us (6%)
  between operations  15 us (1%)
    psum x1, blocking collectives, shards(): power_total = lax.psum(auto_power, 'tm')  300 us
    unnamed x2, waiting for transfers between devices  287 us
    convert_element_type x1, other arithmetic, morlet_parts(): return (real_part.astype(jnp.bfloat16), imag_part.astype(jnp.bfloat16))  147 us
    all_gather x1, blocking collectives, shards(): power_groups = lax.all_gather(power_total, 'chan', axis=0, tiled=True)  61.3 us
    all_to_all x1, starting transfers between devices, shards(): lax.all_to_all(summed, 'chan', split_axis=0, concat_axis=3, tiled=True)  49.6 us
    ppermute x8, waiting for transfers between devices, from_behind(): lax.ppermute(array, axis, [(i, (i + by) % peers) for i in range(peers)])  25.2 us
  transfers between devices with their start and end apart: 10, of which 5 were waited for; matrix products, arithmetic and copies ran while one was open for 17% of the time, Pallas kernels for 0%

commit v1 on v0

--- a/solution.py
+++ b/solution.py
@@ -4,6 +4,7 @@
 import numpy as np
 from jax import lax
 from jax.sharding import PartitionSpec as P
+from jax.lax import all_to_all, psum
 
 NS = 32
 BLK = 128
@@ -101,7 +102,16 @@
         2, 3, 0, 1
     )
     summed = lax.psum_scatter(partial_value, "tm", scatter_dimension=1, tiled=True)
-    owned = lax.all_to_all(summed, "chan", split_axis=0, concat_axis=3, tiled=True)
+    manage_counts = lambda raw, dev_axis: jnp.concatenate(
+        all_to_all(
+            jnp.stack(jnp.split(raw, psum(1, axis_name=dev_axis), axis=0)),
+            axis_name=dev_axis,
+            split_axis=0,
+            concat_axis=0,
+        ),
+        axis=3,
+    )
+    owned = manage_counts(summed, dev_axis="chan")
     owned = owned[:, :, :, position] / ntime
     slots_local = owned.shape[1]
     slot_index = time_index * slots_local + jnp.arange(slots_local, dtype=jnp.int32)

time: 1020 us -> 688 us (0.67)
  waiting for transfers between devices: 314 us -> 26.8 us
  starting transfers between devices: 64.3 us -> 18 us
    unnamed x2 -> x1, waiting for transfers between devices: 287 us -> 0.02 us
    all_to_all x1, starting transfers between devices: 49.6 us -> 3.38 us  [shards(): all_to_all(jnp.stack(jnp.split(raw, psum(1, axis_name=dev_axis), axis=0))...]
  transfers between devices with their start and end apart: 10 -> 10, of which waited for: 5 -> 4; matrix products, arithmetic and copies ran while one was open for 17% -> 26% of each run, Pallas kernels for 0% -> 0%
where the time goes in v1:
time: 688 us; the launch traced here: 687 us
  blocking collectives  369 us (54%)
  other arithmetic  167 us (24%)
  local copies, waits for them, and re-layouts  85.8 us (12%)
  waiting for transfers between devices  26.8 us (4%)
  starting transfers between devices  18 us (3%)
  between operations  14.3 us (2%)
    psum x1, blocking collectives, shards(): power_total = lax.psum(auto_power, 'tm')  302 us
    convert_element_type x1, other arithmetic, morlet_parts(): return (real_part.astype(jnp.bfloat16), imag_part.astype(jnp.bfloat16))  147 us
    all_gather x1, blocking collectives, shards(): power_groups = lax.all_gather(power_total, 'chan', axis=0, tiled=True)  59.1 us
    ppermute x8, waiting for transfers between devices, from_behind(): lax.ppermute(array, axis, [(i, (i + by) % peers) for i in range(peers)])  25.2 us
    reshape x1, local copies, waits for them, and re-layouts, pair_spectra(): real_part.reshape(scale_count, -1)  17.3 us
    reshape x1, local copies, waits for them, and re-layouts, pair_spectra(): imag_part.reshape(scale_count, -1)  16.2 us
    gather x1, local copies, waits for them, and re-layouts, pair_spectra(): jnp.take(imag_part.reshape(scale_count, -1), flat_index, axis=1)  16 us
    gather x1, local copies, waits for them, and re-layouts, pair_spectra(): jnp.take(real_part.reshape(scale_count, -1), flat_index, axis=1)  16 us
  transfers between devices with their start and end apart: 10, of which 4 were waited for; matrix products, arithmetic and copies ran while one was open for 26% of the time, Pallas kernels for 0%

profile of v1, /device:TPU:1, one launch (start us, length us, event | category | flops | bytes accessed | tf_op | source)
XLA Modules:
  0.0 686.8 jit_solution(315308960189223498)
XLA Ops:
  8.0 8.3 %all_gather.6 = bf16[256,128]{1,0:T(8,128)(2,1)S(1)} all-gather(bf16[64,128]{1,0:T(8,128)(2,1)S(1)} %convert_element_type.43), channel_id=1, replica_groups=mesh['tm'=64,'chan'=4] {'chan'}, dimensions={0}, use_global_device_ids=true | all-gather | bytes 81920 | tf_op jit(solution)/shard_map/all_gather | solution.py:81
  16.4 6.4 collective-permute-start.7
  22.8 1.2 collective-permute-start.6
  24.0 5.5 collective-permute-start.5
  31.4 1.2 dynamic_slice.16
  33.6 147.0 %fusion.2 = (bf16[8,1,9,128,128]{4,1,0,3,2:T(2,128)(2,1)S(1)}, bf16[8,1,9,128,128]{4,1,0,3,2:T(2,128)(2,1)S(1)}) fusion(s32[9,128,128]{2,1,0:T(8,128)S(1)} %get-tuple-element.20, s32[8]{0:T(128)S(1)} %broadcast_multiply_fusion.1, f32[8]{0:T(128)S(1)} %get-tuple-element.24, f32[9,128,128]{2,1,0:T(8,128)S(1)} %get-tuple-element.19, f32[8]{0:T(128)S(1)} %get-tuple-element.23), kind=kLoop, calls=%fused_computation.13 | loop fusion | flops 14155776 | bytes 5898336 | tf_op jit(solution)/shard_map/vmap()/convert_element_type | solution.py:29
  180.7 11.7 %maximum_bitcast_fusion = bf16[9,128,8,2,128]{4,3,2,1,0:T(2,128)(2,1)} fusion(bf16[8,1,9,128,128]{4,1,0,3,2:T(2,128)(2,1)S(1)} %get-tuple-element.14, bf16[8,1,9,128,128]{4,1,0,3,2:T(2,128)(2,1)S(1)} %get-tuple-element.13), kind=kLoop, calls=%fused_computation.15 | loop fusion | flops 9437184 | bytes 9437184 | tf_op jit(solution)/shard_map/transpose | solution.py:52
  192.4 8.8 %reshape.238 = bf16[1152,2048]{1,0:T(8,128)(2,1)} reshape(bf16[9,128,8,2,128]{4,3,2,1,0:T(2,128)(2,1)} %maximum_bitcast_fusion) | data formatting | bytes 9437184 | tf_op jit(solution)/shard_map/reshape | solution.py:52
  202.8 7.6 %collective-permute-done.1 = bf16[256,128]{0,1:T(8,128)(2,1)S(1)} collective-permute-done((bf16[256,128]{0,1:T(8,128)(2,1)S(1)}, bf16[256,128]{0,1:T(8,128)(2,1)S(1)}, u32[]{:S(2)}, u32[]{:S(2)}) %collective-permute-start.1) | collective-permute-done | bytes 65568 | tf_op jit(solution)/shard_map/ppermute | solution.py:17
  210.4 9.1 %collective-permute-done.2 = bf16[256,128]{0,1:T(8,128)(2,1)S(1)} collective-permute-done((bf16[256,128]{0,1:T(8,128)(2,1)S(1)}, bf16[256,128]{0,1:T(8,128)(2,1)S(1)}, u32[]{:S(2)}, u32[]{:S(2)}) %collective-permute-start.2) | collective-permute-done | bytes 65568 | tf_op jit(solution)/shard_map/ppermute | solution.py:17
  219.9 8.4 %collective-permute-done.3 = bf16[256,128]{0,1:T(8,128)(2,1)S(1)} collective-permute-done((bf16[256,128]{0,1:T(8,128)(2,1)S(1)}, bf16[256,128]{0,1:T(8,128)(2,1)S(1)}, u32[]{:S(2)}, u32[]{:S(2)}) %collective-permute-start.3) | collective-permute-done | bytes 65568 | tf_op jit(solution)/shard_map/ppermute | solution.py:17
  228.5 3.9 convolution_convert_fusion
  233.4 1.3 fusion.14
  234.7 2.0 slice_add_fusion
  236.7 17.3 %copy.85 = f32[8,256,256]{0,2,1:T(8,128)} copy(f32[8,256,256]{2,1,0:T(8,128)} %get-tuple-element.11) | data formatting | bytes 4194304 | tf_op jit(solution)/shard_map/reshape | solution.py:68
  253.9 16.2 %copy.86 = f32[8,256,256]{0,2,1:T(8,128)} copy(f32[8,256,256]{2,1,0:T(8,128)S(1)} %get-tuple-element.12) | data formatting | bytes 4194304 | tf_op jit(solution)/shard_map/reshape | solution.py:69
  270.1 16.0 %gather_fusion.6 = f32[2048,8]{1,0:T(8,128)S(1)} fusion(f32[8,65536]{0,1:T(8,128)} %bitcast.81, s32[2048]{0:T(1024)S(1)} %fusion.9), kind=kCustom, calls=%fused_computation.clone | custom fusion | bytes 139264 | tf_op jit(solution)/shard_map/jit(_take)/gather | solution.py:68
  286.2 16.0 %gather_fusion.7 = f32[2048,8]{1,0:T(8,128)S(1)} fusion(f32[8,65536]{0,1:T(8,128)} %bitcast.82, s32[2048]{0:T(1024)S(1)} %fusion.9), kind=kCustom, calls=%fused_computation.1.clone | custom fusion | bytes 139264 | tf_op jit(solution)/shard_map/jit(_take)/gather | solution.py:69
  302.6 1.5 maximum_bitcast_fusion.1
  304.8 2.3 gather_fusion.2
  307.1 301.9 %psum.7 = f32[8,256]{0,1:T(8,128)S(1)} all-reduce(f32[8,256]{0,1:T(8,128)S(1)} %bitcast.88), channel_id=1, replica_groups=mesh['tm'=64,'chan'=4] {'tm'}, use_global_device_ids=true, to_apply=%region_1.3 | all-reduce | flops 2048 | bytes 16384 | tf_op jit(solution)/shard_map/psum | solution.py:121
  609.0 59.1 %all_gather.7 = f32[32,256]{1,0:T(8,128)S(1)} all-gather(f32[8,256]{1,0:T(8,128)S(1)} %copy.78), channel_id=1, replica_groups=mesh['tm'=64,'chan'=4] {'chan'}, dimensions={0}, use_global_device_ids=true | all-gather | bytes 40960 | tf_op jit(solution)/shard_map/all_gather | solution.py:122
  670.1 3.4 all-to-all-start
  674.9 1.6 all-to-all-done
  (73 shorter events, 14.6 us)
Async XLA Ops:
  7.2 25.5 %copy-start = (s32[32]{0:T(128)S(1)}, s32[32]{0:T(128)}, u32[]{:S(2)}) copy-start(s32[32]{0:T(128)} %param.11) | copy-start | bytes 388
  7.2 661.5 %reduce-scatter.2.cloned.1.call-start = ((), (), s32[]{:S(2)}) async-start(), calls=%async_computation.2 | async-start | bytes 2129920 | tf_op jit(solution)/shard_map/reduce_scatter | solution.py:104
  16.4 212.1 %collective-permute-start.7 = (bf16[256,128]{0,1:T(8,128)(2,1)S(1)}, bf16[256,128]{0,1:T(8,128)(2,1)S(1)}, u32[]{:S(2)}, u32[]{:S(2)}) collective-permute-start(bf16[256,128]{0,1:T(8,128)(2,1)S(1)} %copy.61), channel_id=1, source_target_pairs={{0,240},{4,244},{8,248},{12,252},{16,0},{20,4},{24,8},{28,12},{32,... | collective-permute-start | bytes 196616 | tf_op jit(solution)/shard_map/ppermute | solution.py:17
  22.8 205.7 %collective-permute-start.6 = (bf16[256,128]{0,1:T(8,128)(2,1)S(1)}, bf16[256,128]{0,1:T(8,128)(2,1)S(1)}, u32[]{:S(2)}, u32[]{:S(2)}) collective-permute-start(bf16[256,128]{0,1:T(8,128)(2,1)S(1)} %copy.61), channel_id=1, source_target_pairs={{0,244},{4,248},{8,252},{12,0},{16,4},{20,8},{24,12},{28,16},{32,2... | collective-permute-start | bytes 196616 | tf_op jit(solution)/shard_map/ppermute | solution.py:17
  24.0 204.4 %collective-permute-start.5 = (bf16[256,128]{0,1:T(8,128)(2,1)S(1)}, bf16[256,128]{0,1:T(8,128)(2,1)S(1)}, u32[]{:S(2)}, u32[]{:S(2)}) collective-permute-start(bf16[256,128]{0,1:T(8,128)(2,1)S(1)} %copy.61), channel_id=1, source_target_pairs={{0,248},{4,252},{8,0},{12,4},{16,8},{20,12},{24,16},{28,20},{32,24... | collective-permute-start | bytes 196616 | tf_op jit(solution)/shard_map/ppermute | solution.py:17
  29.5 198.8 %collective-permute-start.4 = (bf16[256,128]{0,1:T(8,128)(2,1)S(1)}, bf16[256,128]{0,1:T(8,128)(2,1)S(1)}, u32[]{:S(2)}, u32[]{:S(2)}) collective-permute-start(bf16[256,128]{0,1:T(8,128)(2,1)S(1)} %copy.61), channel_id=1, source_target_pairs={{0,252},{4,0},{8,4},{12,8},{16,12},{20,16},{24,20},{28,24},{32,28}... | collective-permute-start | bytes 196616 | tf_op jit(solution)/shard_map/ppermute | solution.py:17
  30.6 172.1 %collective-permute-start = (bf16[256,128]{0,1:T(8,128)(2,1)S(1)}, bf16[256,128]{0,1:T(8,128)(2,1)S(1)}, u32[]{:S(2)}, u32[]{:S(2)}) collective-permute-start(bf16[256,128]{0,1:T(8,128)(2,1)S(1)} %copy.61), channel_id=1, source_target_pairs={{0,16},{4,20},{8,24},{12,28},{16,32},{20,36},{24,40},{28,44},{32,4... | collective-permute-start | bytes 196616 | tf_op jit(solution)/shard_map/ppermute | solution.py:17
  202.7 7.6 %collective-permute-start.1 = (bf16[256,128]{0,1:T(8,128)(2,1)S(1)}, bf16[256,128]{0,1:T(8,128)(2,1)S(1)}, u32[]{:S(2)}, u32[]{:S(2)}) collective-permute-start(bf16[256,128]{0,1:T(8,128)(2,1)S(1)} %copy.61), channel_id=1, source_target_pairs={{0,12},{4,16},{8,20},{12,24},{16,28},{20,32},{24,36},{28,40},{32,4... | collective-permute-start | bytes 196616 | tf_op jit(solution)/shard_map/ppermute | solution.py:17
  210.4 9.1 %collective-permute-start.2 = (bf16[256,128]{0,1:T(8,128)(2,1)S(1)}, bf16[256,128]{0,1:T(8,128)(2,1)S(1)}, u32[]{:S(2)}, u32[]{:S(2)}) collective-permute-start(bf16[256,128]{0,1:T(8,128)(2,1)S(1)} %copy.61), channel_id=1, source_target_pairs={{0,8},{4,12},{8,16},{12,20},{16,24},{20,28},{24,32},{28,36},{32,40... | collective-permute-start | bytes 196616 | tf_op jit(solution)/shard_map/ppermute | solution.py:17
  219.5 8.8 %collective-permute-start.3 = (bf16[256,128]{0,1:T(8,128)(2,1)S(1)}, bf16[256,128]{0,1:T(8,128)(2,1)S(1)}, u32[]{:S(2)}, u32[]{:S(2)}) collective-permute-start(bf16[256,128]{0,1:T(8,128)(2,1)S(1)} %copy.61), channel_id=1, source_target_pairs={{0,4},{4,8},{8,12},{12,16},{16,20},{20,24},{24,28},{28,32},{32,36}... | collective-permute-start | bytes 196616 | tf_op jit(solution)/shard_map/ppermute | solution.py:17
  302.2 377.7 %copy-start.1 = (s32[32]{0:T(128)S(1)}, s32[32]{0:T(128)}, u32[]{:S(2)}) copy-start(s32[32]{0:T(128)} %param.11) | copy-start | bytes 388
  670.1 6.4 all-to-all-start
Sparse Core Ops, SparseCore 0:
  304.2 311.5 reduce-scatter.1
